TPU v7x, 32 devices: a whole 2x2x4 slice. The times are simulated.
32 devices in a mesh: groups: 2 (over x), blk: 16 (over z, y, core).
Axes of the slice: x: 2, y: 2, z: 4, core: 2. Of those that a mesh axis runs over, the one named last changes fastest.
Arguments:
- layer_input_tokens: bfloat16 [384, 8192], P('groups', 'blk'), parts along dimension 0, may hold values from -6 to 6
- input_norm_gain: float32 [8192], replicated, may hold values from 0.5 to 1.5
- query_weight: bfloat16 [8192, 8192], P(None, 'blk'), may hold values from -0.0625 to 0.0625
- key_value_weight: bfloat16 [8192, 2048], P(None, 'blk'), may hold values from -0.0625 to 0.0625
- output_weight: bfloat16 [8192, 8192], P(None, 'blk'), may hold values from -0.5 to 0.5
- adapter_down_weight: bfloat16 [16, 64, 8192], P('blk'), may hold values from -0.0625 to 0.0625
- adapter_up_weight: bfloat16 [16, 64, 8192], P(None, None, 'blk'), may hold values from -0.75 to 0.75
- key_value_page_pool: bfloat16 [512, 128, 2048], P(('groups', 'blk')), parts along dimension 0, may hold values from -240 to 240
- request_adapter: int32 [128], P('groups'), parts along dimension 0, may hold values from 0 to 15
- adapter_storage_slot: int32 [16], replicated, may hold values from 0 to 15, each once
- cached_lengths: int32 [128], P('groups'), parts along dimension 0, may hold values from 1 to 512, as said below
- request_page_tables: int32 [128, 4], P('groups'), parts along dimension 0, may hold values from -1 to 255, as said below
Outputs:
- layer_out: bfloat16 [384, 8192], P('groups', 'blk'), parts along dimension 0
There are 2 independent parts, one for each index of `groups`. A program takes and returns all parts, laid end to end along the dimension named above; an argument that names none is the same for every part. Nothing has to cross between parts.
Inputs may be any that keep to these rules, and one draw needn't show every extreme that they name: `cached_lengths`: each request's cached length; the longest is exactly 512. `request_page_tables`: row r holds ceil(cached_lengths[r] / 128) page numbers first and -1 after them; no page is named twice in the whole table.
All inputs are finite; a program needn't handle non-finite values.
Results may differ from a plain program's by a relative error of at most 0.0085.
The roundings to bfloat16 on the way count: a program that leaves them out, or rounds other values in their place, can miss the bound.
Values may be sent and summed in bfloat16 or wider, within the bound.
No kernel may reach another device: no remote copies, remote signals or barrier semaphores. Data moves between devices by JAX's collectives and lax.ppermute only.
A program may use at most 128 MiB of HBM per device.

v0:
```python
import math
import jax
import jax.numpy as jnp
from jax import lax
from jax.sharding import PartitionSpec as P

QUERY_HEADS = 64
KEY_VALUE_HEADS = 8
HEAD_WIDTH = 128
PAGE_LENGTH = 128
NEW_TOKENS = 3
theta_base = 500000.0
neg_large = -1e30


def apply_rotation(values, token_positions, first_col, rot_limit):
    width_cols = values.shape[1]
    columns = first_col + jnp.arange(width_cols, dtype=jnp.int32)
    pair_index = (columns % HEAD_WIDTH // 2).astype(jnp.float32)
    inverse = jnp.exp(pair_index * (-2.0 * math.log(theta_base) / HEAD_WIDTH))
    angles = token_positions[:, None] * inverse[None, :]
    cos_val = jnp.cos(angles[:, 0::2])
    sine_val = jnp.sin(angles[:, 0::2])
    even_part = values[:, 0::2]
    odd_part = values[:, 1::2]
    turned = jnp.stack(
        [even_part * cos_val - odd_part * sine_val, even_part * sine_val + odd_part * cos_val],
        axis=-1,
    ).reshape(values.shape)
    return jnp.where((columns < rot_limit)[None, :], turned, values)


def normalize(layer_input_tokens, input_norm_gain):
    values = layer_input_tokens.astype(jnp.float32)
    mean_square = jnp.mean(values * values, axis=-1, keepdims=True)
    return (values * lax.rsqrt(mean_square + 1e-05) * input_norm_gain[None, :]).astype(jnp.bfloat16)


def positions_of(cached_lengths):
    steps_row = jnp.arange(NEW_TOKENS, dtype=jnp.int32)
    return (
        jnp.repeat(cached_lengths, NEW_TOKENS) + jnp.tile(steps_row, cached_lengths.shape[0])
    ).astype(jnp.float32)


def to_tokens(request_first_layout):
    request_count = request_first_layout.shape[0]
    trailing_shape = request_first_layout.shape[3:]
    query_group_width = QUERY_HEADS // KEY_VALUE_HEADS
    split_head_shape = request_first_layout.reshape(
        (request_count, KEY_VALUE_HEADS, NEW_TOKENS, query_group_width) + trailing_shape
    )
    order_axes = (0, 2, 1, 3) + tuple(range(4, 4 + len(trailing_shape)))
    return split_head_shape.transpose(order_axes).reshape(request_count * NEW_TOKENS, -1)


def butterfly(value, combine):
    size = lax.axis_size("blk")
    step = 1
    while step < size:
        pairs = [(i, i ^ step) for i in range(size)]
        value = combine(value, lax.ppermute(value, "blk", pairs))
        step *= 2
    return value


def local(
    layer_input_tokens,
    input_norm_gain,
    query_weight,
    key_value_weight,
    output_weight,
    adapter_down_weight,
    adapter_up_weight,
    key_value_page_pool,
    request_adapter,
    adapter_storage_slot,
    cached_lengths,
    request_page_tables,
):
    own_index = lax.axis_index("blk")
    gathered = lax.all_gather(layer_input_tokens, "blk", axis=1, tiled=True)
    normalized_input = normalize(gathered, input_norm_gain)
    request_count = cached_lengths.shape[0]
    adapter_total = adapter_storage_slot.shape[0]
    choose = request_adapter[:, None] == jnp.arange(adapter_total, dtype=jnp.int32)[None, :]
    req_slot = jnp.sum(jnp.where(choose, adapter_storage_slot[None, :], 0), axis=1)
    token_cache_slot = jnp.repeat(req_slot, NEW_TOKENS)
    local_token_count = adapter_down_weight.shape[0]
    local_pick = (
        token_cache_slot[:, None] - own_index * local_token_count
        == jnp.arange(local_token_count, dtype=jnp.int32)[None, :]
    )
    output_projected = jnp.einsum(
        "ly,mxy->lmx", normalized_input, adapter_down_weight, preferred_element_type=jnp.float32
    )
    partial_codes = jnp.sum(jnp.where(local_pick[:, :, None], output_projected, 0.0), axis=1)
    adapter_choice_index = butterfly(partial_codes.astype(jnp.bfloat16), jnp.add)
    up_weight_rows = adapter_up_weight[token_cache_slot]
    adapter_query_update = jnp.einsum(
        "gk,gkq->gq", adapter_choice_index, up_weight_rows, preferred_element_type=jnp.float32
    )
    token_positions = positions_of(cached_lengths)
    query_cols = query_weight.shape[1]
    keyval_cols = key_value_weight.shape[1]
    query_part = apply_rotation(
        jnp.dot(normalized_input, query_weight, preferred_element_type=jnp.float32)
        + adapter_query_update,
        token_positions,
        own_index * query_cols,
        QUERY_HEADS * HEAD_WIDTH,
    ).astype(jnp.bfloat16)
    keyval_part = apply_rotation(
        jnp.dot(normalized_input, key_value_weight, preferred_element_type=jnp.float32),
        token_positions,
        own_index * keyval_cols,
        KEY_VALUE_HEADS * HEAD_WIDTH,
    ).astype(jnp.bfloat16)
    joined = lax.all_gather(
        jnp.concatenate([query_part, keyval_part], axis=1), "blk", axis=1, tiled=False
    )
    query_vectors = joined[:, :, :query_cols].reshape(joined.shape[0], -1)
    key_value_rows = joined[:, :, query_cols:].reshape(joined.shape[0], -1)
    query_group_width = QUERY_HEADS // KEY_VALUE_HEADS
    query_feature_width = query_group_width * NEW_TOKENS
    score_scale = 1.0 / math.sqrt(HEAD_WIDTH)
    query_req = (
        query_vectors.reshape(
            request_count, NEW_TOKENS, KEY_VALUE_HEADS, query_group_width, HEAD_WIDTH
        )
        .transpose(0, 2, 1, 3, 4)
        .reshape(request_count, KEY_VALUE_HEADS, query_feature_width, HEAD_WIDTH)
    )
    fresh_token_rows = key_value_rows.reshape(
        request_count, NEW_TOKENS, 2, KEY_VALUE_HEADS, HEAD_WIDTH
    )
    request_page_count = key_value_page_pool.shape[0]
    table_width = request_page_tables.shape[1]
    page_ids = own_index * request_page_count + jnp.arange(request_page_count, dtype=jnp.int32)
    matches = request_page_tables[None, :, :] == page_ids[:, None, None]
    page_owner = jnp.any(matches, axis=2)
    page_live = jnp.any(page_owner, axis=1)
    page_req = jnp.sum(
        jnp.where(page_owner, jnp.arange(request_count, dtype=jnp.int32)[None, :], 0), axis=1
    )
    page_slot = jnp.sum(
        jnp.where(matches, jnp.arange(table_width, dtype=jnp.int32)[None, None, :], 0), axis=(1, 2)
    )
    page_len = jnp.sum(jnp.where(page_owner, cached_lengths[None, :], 0), axis=1)
    key_pos = page_slot[:, None] * PAGE_LENGTH + jnp.arange(PAGE_LENGTH, dtype=jnp.int32)[None, :]
    key_valid = page_live[:, None] & (key_pos < page_len[:, None])
    valid_full = key_valid[:, None, None, :]
    gathered_cache_pages = key_value_page_pool.reshape(
        request_page_count, PAGE_LENGTH, 2, KEY_VALUE_HEADS, HEAD_WIDTH
    )
    query_page = query_req[page_req]
    scores = (
        jnp.einsum(
            "skqd,spkd->skqp",
            query_page,
            gathered_cache_pages[:, :, 0],
            preferred_element_type=jnp.float32,
        )
        * score_scale
    )
    masked = jnp.where(valid_full, scores, neg_large)
    page_peak = jnp.max(masked, axis=-1)
    req_peak = jnp.max(
        jnp.where(page_owner[:, :, None, None], page_peak[:, None], neg_large), axis=0
    )
    fresh_scores = (
        jnp.einsum(
            "rkqd,rjkd->rkqj",
            query_req,
            fresh_token_rows[:, :, 0],
            preferred_element_type=jnp.float32,
        )
        * score_scale
    )
    step_of = jnp.arange(query_feature_width, dtype=jnp.int32) // query_group_width
    fresh_ok = (jnp.arange(NEW_TOKENS, dtype=jnp.int32)[None, :] <= step_of[:, None])[None, None]
    fresh_masked = jnp.where(fresh_ok, fresh_scores, neg_large)
    top_score = butterfly(jnp.maximum(req_peak, jnp.max(fresh_masked, axis=-1)), jnp.maximum)
    weights = jnp.where(valid_full, jnp.exp(masked - top_score[page_req][..., None]), 0.0)
    page_num = jnp.einsum(
        "skqp,spkd->skqd",
        weights.astype(jnp.bfloat16),
        gathered_cache_pages[:, :, 1],
        preferred_element_type=jnp.float32,
    )
    device_count = lax.axis_size("blk")
    head_count = QUERY_HEADS
    owner_cols = query_cols
    owner_heads = max(1, owner_cols // HEAD_WIDTH)
    head_repeat = min(owner_cols, HEAD_WIDTH)
    owner_first_head = [o * owner_cols // HEAD_WIDTH for o in range(device_count)]
    head_pick = jnp.asarray(
        [[first + j for j in range(owner_heads)] for first in owner_first_head], jnp.int32
    )
    slot_num = to_tokens(page_num).reshape(request_page_count, NEW_TOKENS, device_count, owner_cols)
    slot_den = to_tokens(jnp.sum(weights, axis=-1)[..., None]).reshape(
        request_page_count, NEW_TOKENS, head_count
    )
    slot_den_owner = slot_den[:, :, head_pick]
    packed = jnp.concatenate([slot_num, slot_den_owner], axis=3).transpose(2, 0, 1, 3)
    received = lax.all_to_all(packed, "blk", 0, 0, tiled=True)
    group_pages = device_count * request_page_count
    all_page_ids = jnp.arange(group_pages, dtype=jnp.int32)
    all_owner = jnp.any(request_page_tables[None, :, :] == all_page_ids[:, None, None], axis=2)
    pick_req = all_owner.T.astype(jnp.float32)
    summed = jnp.einsum(
        "rp,px->rx", pick_req, received.reshape(group_pages, -1), precision=lax.Precision.HIGHEST
    ).reshape(request_count, NEW_TOKENS, owner_cols + owner_heads)
    fresh_weights = jnp.where(fresh_ok, jnp.exp(fresh_masked - top_score[..., None]), 0.0)
    fresh_num = jnp.einsum(
        "rkqj,rjkd->rkqd",
        fresh_weights.astype(jnp.bfloat16),
        fresh_token_rows[:, :, 1],
        preferred_element_type=jnp.float32,
    )
    fresh_den = jnp.sum(fresh_weights, axis=-1)
    fresh_num_own = lax.dynamic_slice_in_dim(
        to_tokens(fresh_num), own_index * owner_cols, owner_cols, axis=1
    )
    fresh_den_own = lax.dynamic_slice_in_dim(
        to_tokens(fresh_den[..., None]), own_index * owner_cols // HEAD_WIDTH, owner_heads, axis=1
    )
    num_own = summed[:, :, :owner_cols].reshape(request_count * NEW_TOKENS, owner_cols)
    den_own = summed[:, :, owner_cols:].reshape(request_count * NEW_TOKENS, owner_heads)
    totals = den_own + fresh_den_own
    attended_own = ((num_own + fresh_num_own) / jnp.repeat(totals, head_repeat, axis=1)).astype(
        jnp.bfloat16
    )
    attended = lax.all_gather(attended_own, "blk", axis=1, tiled=True)
    return jnp.dot(attended, output_weight, preferred_element_type=jnp.float32).astype(jnp.bfloat16)


def solution(mesh):
    placed = (
        P("groups", "blk"),
        P(),
        P(None, "blk"),
        P(None, "blk"),
        P(None, "blk"),
        P("blk", None, None),
        P(None, None, "blk"),
        P(("groups", "blk"), None, None),
        P("groups"),
        P(),
        P("groups"),
        P("groups", None),
    )
    return jax.shard_map(
        local, mesh=mesh, in_specs=placed, out_specs=P("groups", "blk"), check_vma=False
    )
```

profile of v0, /device:TPU:0, one launch (start us, length us, event | category | flops | bytes accessed | tf_op | source)
XLA Modules:
  0.0 356.7 jit_solution(8480461503229381404)
XLA Ops:
  12.0 7.3 %slice.45 = f32[192,256]{1,0:T(8,128)} slice(f32[192,512]{1,0:T(8,128)S(1)} %broadcast_multiply_fusion), slice={[0:192:1], [0:512:2]} | slice | bytes 393216 | tf_op jit(solution)/shard_map/slice | solution.py:22
  19.3 8.3 %gather_fusion = bf16[192,64,512]{2,1,0:T(8,128)(2,1)} fusion(bf16[16,64,512]{2,1,0:T(8,128)(2,1)S(1)} %copy-done.2, s32[1024]{0:T(1024)S(1)} %pad_clamp_fusion.2), kind=kCustom, calls=%fused_computation | custom fusion | bytes 25166592 | tf_op jit(solution)/shard_map/gather | solution.py:99
  28.7 30.7 %all-gather.5.cloned.1.call-done = bf16[192,8192]{1,0:T(8,128)(2,1)} async-done(((bf16[192,512]{1,0:T(8,128)(2,1)}), bf16[192,8192]{1,0:T(8,128)(2,1)}) %all-gather.5.cloned.1.call-update) | async-done | bytes 3145744 | tf_op jit(solution)/shard_map/all_gather | solution.py:82
  74.2 3.5 collective-permute-done.2
  82.7 6.5 %fusion.48 = f32[192,1,512]{2,1,0:T(1,128)S(1)} fusion(bf16[192,64,1]{1,2,0:T(2,128)(2,1)S(1)} %copy.154, bf16[192,64,512]{2,1,0:T(8,128)(2,1)} %gather_fusion), kind=kOutput, calls=%fused_computation.123 | convolution fusion | flops 12582912 | bytes 13000704 | tf_op jit(solution)/shard_map/gk,gkq->gq/dot_general | solution.py:100
  89.1 5.3 %convolution_add_fusion = f32[192,512]{1,0:T(8,128)S(1)} fusion(bf16[8192,512]{1,0:T(8,128)(2,1)} %param.15, f32[192,1,512]{2,1,0:T(1,128)S(1)} %fusion.48, bf16[192,8192]{1,0:T(8,128)(2,1)S(1)} %copy-done.4, f32[8192]{0:T(1024)S(1)} %copy-done.9, f32[192]{0:T(256)S(1)} %add_rsqrt_fusion), kind=kOutput, calls=%fused_computation.26 | convolution fusion | flops 1617002496 | bytes 12354304 | tf_op jit(solution)/shard_map/dot_general | solution.py:107
  94.4 7.2 %slice.46 = f32[192,256]{1,0:T(8,128)S(1)} slice(f32[192,512]{1,0:T(8,128)S(1)} %convolution_add_fusion), slice={[0:192:1], [1:512:2]} | slice | bytes 393216 | tf_op jit(solution)/shard_map/slice | solution.py:25
  101.6 6.7 %slice.44 = f32[192,256]{1,0:T(8,128)S(1)} slice(f32[192,512]{1,0:T(8,128)S(1)} %convolution_add_fusion), slice={[0:192:1], [0:512:2]} | slice | bytes 393216 | tf_op jit(solution)/shard_map/slice | solution.py:24
  109.8 12.3 %copy.132 = bf16[16,128,2048]{1,2,0:T(8,128)(2,1)} copy(bf16[16,128,2048]{2,1,0:T(8,128)(2,1)} %param.20) | data formatting | bytes 16777216 | tf_op args[7]
  122.7 35.0 %all-gather.9.cloned.1.call-done = bf16[192,10240]{1,0:T(8,128)(2,1)} async-done(((bf16[192,640]{1,0:T(8,128)(2,1)}), bf16[192,10240]{1,0:T(8,128)(2,1)}) %all-gather.9.cloned.1.call-update) | async-done | bytes 3932176 | tf_op jit(solution)/shard_map/all_gather | solution.py:119
  163.8 6.1 %reshape_reshape.12 = bf16[64,3,8,8,128]{4,3,2,1,0:T(8,128)(2,1)} reshape(bf16[192,16,512]{2,1,0:T(8,128)(2,1)} %slice.66) | data formatting | bytes 6291456 | tf_op jit(solution)/shard_map/reshape;reshape | solution.py:128
  169.9 4.2 %copy.181 = bf16[64,3,8,8,128]{4,3,1,2,0:T(8,128)(2,1)} copy(bf16[64,3,8,8,128]{4,3,2,1,0:T(8,128)(2,1)} %reshape_reshape.12) | data formatting | bytes 6291456 | tf_op jit(solution)/shard_map/reshape;reshape | solution.py:128
  176.7 3.5 fusion.46
  182.8 3.7 %fusion.47 = (f32[64,8,24]{2,1,0:T(8,128)S(1)}, f32[64,8,24,3]{2,3,1,0:T(4,128)S(1)}) fusion(bf16[64,3,1,8,128]{4,3,2,1,0:T(8,128)(2,1)S(1)} %get-tuple-element.10, bf16[64,3,8,8,128]{4,3,2,1,0:T(8,128)(2,1)} %reshape_reshape.12, pred[24,3]{0,1:T(4,128)(4,1)S(1)} %iota_compare_fusion.2), kind=kOutput, calls=%fused_computation.122 | convolution fusion | flops 9535488 | bytes 3735624 | tf_op jit(solution)/shard_map/rkqd,rjkd->rkqj/dot_general | solution.py:172
  188.7 7.9 %collective-permute-done.5 = f32[64,8,24]{2,1,0:T(8,128)S(1)} collective-permute-done((f32[64,8,24]{2,1,0:T(8,128)S(1)}, f32[64,8,24]{2,1,0:T(8,128)S(1)}, u32[]{:S(2)}, u32[]{:S(2)}) %collective-permute-start.5) | collective-permute-done | bytes 49184 | tf_op jit(solution)/shard_map/ppermute | solution.py:62
  198.6 5.9 %collective-permute-done.6 = f32[64,8,24]{2,1,0:T(8,128)S(1)} collective-permute-done((f32[64,8,24]{2,1,0:T(8,128)S(1)}, f32[64,8,24]{2,1,0:T(8,128)S(1)}, u32[]{:S(2)}, u32[]{:S(2)}) %collective-permute-start.6) | collective-permute-done | bytes 49184 | tf_op jit(solution)/shard_map/ppermute | solution.py:62
  206.6 11.4 %collective-permute-done.7 = f32[64,8,24]{2,1,0:T(8,128)S(1)} collective-permute-done((f32[64,8,24]{2,1,0:T(8,128)S(1)}, f32[64,8,24]{2,1,0:T(8,128)S(1)}, u32[]{:S(2)}, u32[]{:S(2)}) %collective-permute-start.7) | collective-permute-done | bytes 49184 | tf_op jit(solution)/shard_map/ppermute | solution.py:62
  219.6 5.8 %fusion.5 = f32[16,8,3,8,128]{4,3,2,1,0:T(8,128)} fusion(bf16[16,128,2,8,128]{1,4,3,2,0:T(8,128)(2,1)} %bitcast.110, f32[16,8,24,128]{3,2,1,0:T(8,128)S(1)} %get-tuple-element.20, f32[16,8,24]{2,1,0:T(8,128)S(1)} %gather_fusion.2, pred[16,128]{1,0:T(8,128)(4,1)S(1)} %fusion.26), kind=kOutput, calls=%fused_computation.21 | convolution fusion | flops 101842944 | bytes 7354368 | tf_op jit(solution)/shard_map/skqp,spkd->skqd/dot_general | solution.py:185
  234.0 3.7 %all-to-all-start = ((f32[16,16,3,516]{3,1,2,0:T(8,128)}), f32[16,16,3,516]{3,1,2,0:T(8,128)S(1)}, u32[]{:S(2)}, u32[]{:S(2)}) async-start(f32[16,16,3,516]{3,1,2,0:T(8,128)} %copy.143), calls=%async_computation | async-start | bytes 3932160 | tf_op jit(solution)/shard_map/all_to_all | solution.py:206
  246.4 3.4 copy.180
  249.8 7.2 %reshape.298 = f32[192,8192]{1,0:T(8,128)} reshape(f32[64,3,8,8,128]{4,3,2,1,0:T(8,128)} %bitcast.111) | data formatting | bytes 12582912 | tf_op jit(solution)/shard_map/reshape | solution.py:54
  257.0 19.5 %all-to-all-done = f32[16,16,3,516]{3,1,2,0:T(8,128)S(1)} async-done(((f32[16,16,3,516]{3,1,2,0:T(8,128)}), f32[16,16,3,516]{3,1,2,0:T(8,128)S(1)}, u32[]{:S(2)}, u32[]{:S(2)}) %all-to-all-start) | async-done | bytes 1585184 | tf_op jit(solution)/shard_map/all_to_all | solution.py:206
  289.7 53.3 %all-gather.7.cloned.1.call-done = bf16[192,8192]{1,0:T(8,128)(2,1)} async-done(((bf16[192,512]{1,0:T(8,128)(2,1)}), bf16[192,8192]{1,0:T(8,128)(2,1)}) %all-gather.7.cloned.1.call-update) | async-done | bytes 3145744 | tf_op jit(solution)/shard_map/all_gather | solution.py:234
  343.0 6.9 %convolution_convert_fusion = bf16[192,512]{1,0:T(8,128)(2,1)} fusion(bf16[192,8192]{1,0:T(8,128)(2,1)} %all-gather.7.cloned.1.call-done, bf16[8192,512]{1,0:T(8,128)(2,1)} %param.17), kind=kOutput, calls=%fused_computation.27 | convolution fusion | flops 1610711040 | bytes 11730944 | tf_op jit(solution)/shard_map/dot_general | solution.py:235
  (139 shorter events, 77.5 us)
Async XLA Ops:
  6.5 58.5 %copy-start = (bf16[8192,128]{1,0:T(8,128)(2,1)S(1)}, bf16[8192,128]{1,0:T(8,128)(2,1)}, u32[]{:S(2)}) copy-start(bf16[8192,128]{1,0:T(8,128)(2,1)} %param.16) | copy-start | bytes 6291460
  6.5 12.7 %copy-start.2 = (bf16[16,64,512]{2,1,0:T(8,128)(2,1)S(1)}, bf16[16,64,512]{2,1,0:T(8,128)(2,1)}, u32[]{:S(2)}) copy-start(bf16[16,64,512]{2,1,0:T(8,128)(2,1)} %param.19) | copy-start | bytes 3145732
  6.5 52.9 %all-gather.5.cloned.1.call-start = ((), (), s32[]{:S(2)}) async-start(), calls=%async_computation.1 | async-start | bytes 3342336 | tf_op jit(solution)/shard_map/all_gather | solution.py:82
  7.3 150.4 %all-gather.9.cloned.1.call-start = ((), (), s32[]{:S(2)}) async-start(), calls=%async_computation.3 | async-start | bytes 4177920 | tf_op jit(solution)/shard_map/all_gather | solution.py:119
  19.2 8.4 %copy-start.6 = (f32[192,64]{1,0:T(8,128)S(1)}, f32[192,64]{1,0:T(8,128)}, u32[]{:S(2)}) copy-start(f32[192,64]{1,0:T(8,128)} %slice.48) | copy-start | bytes 147460
  19.3 8.8 %copy-start.5 = (f32[192,256]{1,0:T(8,128)S(1)}, f32[192,256]{1,0:T(8,128)}, u32[]{:S(2)}) copy-start(f32[192,256]{1,0:T(8,128)} %slice.45) | copy-start | bytes 589828
  27.6 34.6 %copy-start.9 = (f32[8192]{0:T(1024)S(1)}, f32[8192]{0:T(1024)}, u32[]{:S(2)}) copy-start(f32[8192]{0:T(1024)} %param.14) | copy-start | bytes 98308
  59.5 2.8 copy-start.3
  64.7 4.9 %collective-permute-start = (bf16[192,64]{0,1:T(8,128)(2,1)S(1)}, bf16[192,64]{0,1:T(8,128)(2,1)S(1)}, u32[]{:S(2)}, u32[]{:S(2)}) collective-permute-start(bf16[192,64]{0,1:T(8,128)(2,1)S(1)} %fusion.9), channel_id=1, source_target_pairs={{0,1},{1,0},{2,3},{3,2},{4,5},{5,4},{6,7},{7,6},{8,9},{9,8},{10,11... | collective-permute-start | bytes 73736 | tf_op jit(solution)/shard_map/ppermute | solution.py:62
  69.6 4.0 %collective-permute-start.1 = (bf16[192,64]{0,1:T(8,128)(2,1)S(1)}, bf16[192,64]{0,1:T(8,128)(2,1)S(1)}, u32[]{:S(2)}, u32[]{:S(2)}) collective-permute-start(bf16[192,64]{0,1:T(8,128)(2,1)S(1)} %add.180), channel_id=1, source_target_pairs={{0,2},{1,3},{2,0},{3,1},{4,6},{5,7},{6,4},{7,5},{8,10},{9,11},{10,... | collective-permute-start | bytes 73736 | tf_op jit(solution)/shard_map/ppermute | solution.py:62
  73.6 4.0 %collective-permute-start.2 = (bf16[192,64]{0,1:T(8,128)(2,1)S(1)}, bf16[192,64]{0,1:T(8,128)(2,1)S(1)}, u32[]{:S(2)}, u32[]{:S(2)}) collective-permute-start(bf16[192,64]{0,1:T(8,128)(2,1)S(1)} %add.181), channel_id=1, source_target_pairs={{0,4},{1,5},{2,6},{3,7},{4,0},{5,1},{6,2},{7,3},{8,12},{9,13},{10,... | collective-permute-start | bytes 73736 | tf_op jit(solution)/shard_map/ppermute | solution.py:62
  77.6 4.9 %collective-permute-start.3 = (bf16[192,64]{0,1:T(8,128)(2,1)S(1)}, bf16[192,64]{0,1:T(8,128)(2,1)S(1)}, u32[]{:S(2)}, u32[]{:S(2)}) collective-permute-start(bf16[192,64]{0,1:T(8,128)(2,1)S(1)} %add.182), channel_id=1, source_target_pairs={{0,8},{1,9},{2,10},{3,11},{4,12},{5,13},{6,14},{7,15},{8,0},{9,1},... | collective-permute-start | bytes 73736 | tf_op jit(solution)/shard_map/ppermute | solution.py:62
  82.6 6.5 %copy-start.4 = (bf16[192,8192]{1,0:T(8,128)(2,1)S(1)}, bf16[192,8192]{1,0:T(8,128)(2,1)}, u32[]{:S(2)}) copy-start(bf16[192,8192]{1,0:T(8,128)(2,1)} %all-gather.5.cloned.1.call-done) | copy-start | bytes 9437188
  109.8 12.3 %copy-start.7 = (s32[64,4]{0,1:T(4,128)S(1)}, s32[64,4]{0,1:T(4,128)}, u32[]{:S(2)}) copy-start(s32[64,4]{0,1:T(4,128)} %param.24) | copy-start | bytes 3076
  109.8 12.5 %copy-start.8 = (s32[64]{0:T(128)S(1)}, s32[64]{0:T(128)}, u32[]{:S(2)}) copy-start(s32[64]{0:T(128)} %param.23) | copy-start | bytes 772
  186.5 1.6 collective-permute-start.4
  188.1 8.5 %collective-permute-start.5 = (f32[64,8,24]{2,1,0:T(8,128)S(1)}, f32[64,8,24]{2,1,0:T(8,128)S(1)}, u32[]{:S(2)}, u32[]{:S(2)}) collective-permute-start(f32[64,8,24]{2,1,0:T(8,128)S(1)} %max.16), channel_id=1, source_target_pairs={{0,2},{1,3},{2,0},{3,1},{4,6},{5,7},{6,4},{7,5},{8,10},{9,11},{10,... | collective-permute-start | bytes 147464 | tf_op jit(solution)/shard_map/ppermute | solution.py:62
  196.7 7.9 %collective-permute-start.6 = (f32[64,8,24]{2,1,0:T(8,128)S(1)}, f32[64,8,24]{2,1,0:T(8,128)S(1)}, u32[]{:S(2)}, u32[]{:S(2)}) collective-permute-start(f32[64,8,24]{2,1,0:T(8,128)S(1)} %max.17), channel_id=1, source_target_pairs={{0,4},{1,5},{2,6},{3,7},{4,0},{5,1},{6,2},{7,3},{8,12},{9,13},{10,... | collective-permute-start | bytes 147464 | tf_op jit(solution)/shard_map/ppermute | solution.py:62
  204.6 13.5 %collective-permute-start.7 = (f32[64,8,24]{2,1,0:T(8,128)S(1)}, f32[64,8,24]{2,1,0:T(8,128)S(1)}, u32[]{:S(2)}, u32[]{:S(2)}) collective-permute-start(f32[64,8,24]{2,1,0:T(8,128)S(1)} %max.18), channel_id=1, source_target_pairs={{0,8},{1,9},{2,10},{3,11},{4,12},{5,13},{6,14},{7,15},{8,0},{9,1},... | collective-permute-start | bytes 147464 | tf_op jit(solution)/shard_map/ppermute | solution.py:62
  234.0 42.5 %all-to-all-start = ((f32[16,16,3,516]{3,1,2,0:T(8,128)}), f32[16,16,3,516]{3,1,2,0:T(8,128)S(1)}, u32[]{:S(2)}, u32[]{:S(2)}) async-start(f32[16,16,3,516]{3,1,2,0:T(8,128)} %copy.143), calls=%async_computation | async-start | bytes 3932160 | tf_op jit(solution)/shard_map/all_to_all | solution.py:206
  237.7 105.3 %all-gather.7.cloned.1.call-start = ((), (), s32[]{:S(2)}) async-start(), calls=%async_computation.2 | async-start | bytes 3342336 | tf_op jit(solution)/shard_map/all_gather | solution.py:234
  343.0 6.9 %copy-start.1 = (bf16[8192,128]{1,0:T(8,128)(2,1)S(1)}, bf16[8192,128]{1,0:T(8,128)(2,1)}, u32[]{:S(2)}) copy-start(bf16[8192,128]{1,0:T(8,128)(2,1)} %param.16) | copy-start | bytes 6291460
Sparse Core Ops, SparseCore 0:
  9.5 49.8 all-gather.4
  109.9 47.7 all-gather.8
  289.8 53.1 all-gather.6
where the time goes:
time: 362 us; the launch traced here: 357 us
  waiting for transfers between devices  175 us (48%)
  local copies, waits for them, and re-layouts  103 us (28%)
  matrix products  39.1 us (11%)
  between operations  13.9 us (4%)
  other arithmetic  12.9 us (4%)
  starting transfers between devices  12.4 us (3%)
    all_gather x1, waiting for transfers between devices, local(): attended = lax.all_gather(attended_own, 'blk', axis=1, tiled=True)  53.3 us
    ppermute x8, waiting for transfers between devices, butterfly(): value = combine(value, lax.ppermute(value, 'blk', pairs))  35.9 us
    all_gather x1, waiting for transfers between devices, local(): lax.all_gather(jnp.concatenate([query_part, keyval_part], axis=1), 'blk',...  35 us
    all_gather x1, waiting for transfers between devices, local(): gathered = lax.all_gather(layer_input_tokens, 'blk', axis=1, tiled=True)  30.7 us
    all_to_all x1, waiting for transfers between devices, local(): received = lax.all_to_all(packed, 'blk', 0, 0, tiled=True)  19.5 us
    unnamed x23, local copies, waits for them, and re-layouts  15.3 us
    another operation x2, local copies, waits for them, and re-layouts, local(): query_vectors.reshape(request_count, NEW_TOKENS, KEY_VALUE_HEADS, query_g...  10.3 us
    slice x2, local copies, waits for them, and re-layouts, apply_rotation(): cos_val = jnp.cos(angles[:, 0::2])  9.56 us
  transfers between devices with their start and end apart: 12, of which 11 were waited for; matrix products, arithmetic and copies ran while one was open for 16% of the time, Pallas kernels for 0%

commit v1 on v0

--- a/solution.py
+++ b/solution.py
@@ -11,6 +11,17 @@
 NEW_TOKENS = 3
 theta_base = 500000.0
 neg_large = -1e30
+
+
+def gather_around(shard, axis, dim):
+    ways = lax.axis_size(axis)
+    pieces = [shard]
+    for far in range(1, ways):
+        pieces.append(
+            lax.ppermute(pieces[far - 1], axis, [(d, (d - 1) % ways) for d in range(ways)])
+        )
+    line = jnp.concatenate(pieces, axis=dim)
+    return jnp.roll(line, lax.axis_index(axis) * shard.shape[dim], axis=dim)
 
 
 def apply_rotation(values, token_positions, first_col, rot_limit):
@@ -79,7 +90,7 @@
     request_page_tables,
 ):
     own_index = lax.axis_index("blk")
-    gathered = lax.all_gather(layer_input_tokens, "blk", axis=1, tiled=True)
+    gathered = gather_around(layer_input_tokens, "blk", 1)
     normalized_input = normalize(gathered, input_norm_gain)
     request_count = cached_lengths.shape[0]
     adapter_total = adapter_storage_slot.shape[0]

time: 362 us -> 436 us (1.20)
  starting transfers between devices: 12.4 us -> 72.5 us
  local copies, waits for them, and re-layouts: 103 us -> 113 us
    ppermute x0 -> x15, starting transfers between devices: none -> 61.7 us  [gather_around(): lax.ppermute(pieces[far - 1], axis, [(d, (d - 1) % ways) for d in range(w...]
    ppermute x0 -> x15, waiting for transfers between devices: none -> 30.9 us  [gather_around(): lax.ppermute(pieces[far - 1], axis, [(d, (d - 1) % ways) for d in range(w...]
    all_gather x1 -> x0, waiting for transfers between devices: 30.7 us -> none  [local(): gathered = lax.all_gather(layer_input_tokens, 'blk', axis=1, tiled=True)]
    unnamed x23 -> x56, local copies, waits for them, and re-layouts: 15.3 us -> 23.7 us
  transfers between devices with their start and end apart: 12 -> 26, of which waited for: 11 -> 23; matrix products, arithmetic and copies ran while one was open for 16% -> 15% of each run, Pallas kernels for 0% -> 0%
where the time goes in v1:
time: 436 us; the launch traced here: 428 us
  waiting for transfers between devices  179 us (41%)
  local copies, waits for them, and re-layouts  113 us (26%)
  starting transfers between devices  72.5 us (17%)
  matrix products  38.4 us (9%)
  between operations  14.5 us (3%)
  other arithmetic  10.9 us (2%)
    ppermute x15, starting transfers between devices, gather_around(): lax.ppermute(pieces[far - 1], axis, [(d, (d - 1) % ways) for d in range(w...  61.7 us
    all_gather x1, waiting for transfers between devices, local(): attended = lax.all_gather(attended_own, 'blk', axis=1, tiled=True)  53.3 us
    all_gather x1, waiting for transfers between devices, local(): lax.all_gather(jnp.concatenate([query_part, keyval_part], axis=1), 'blk',...  37.6 us
    ppermute x8, waiting for transfers between devices, butterfly(): value = combine(value, lax.ppermute(value, 'blk', pairs))  37.4 us
    ppermute x15, waiting for transfers between devices, gather_around(): lax.ppermute(pieces[far - 1], axis, [(d, (d - 1) % ways) for d in range(w...  30.9 us
    unnamed x56, local copies, waits for them, and re-layouts  23.7 us
    all_to_all x1, waiting for transfers between devices, local(): received = lax.all_to_all(packed, 'blk', 0, 0, tiled=True)  19.5 us
    another operation x2, local copies, waits for them, and re-layouts, local(): query_vectors.reshape(request_count, NEW_TOKENS, KEY_VALUE_HEADS, query_g...  10.3 us
  transfers between devices with their start and end apart: 26, of which 23 were waited for; matrix products, arithmetic and copies ran while one was open for 15% of the time, Pallas kernels for 0%

profile of v1, /device:TPU:0, one launch (start us, length us, event | category | flops | bytes accessed | tf_op | source)
XLA Modules:
  0.0 428.1 jit_solution(4028183116907880000)
XLA Ops:
  6.5 5.4 %collective-permute-start = (bf16[192,512]{1,0:T(8,128)(2,1)}, bf16[192,512]{1,0:T(8,128)(2,1)S(1)}, u32[]{:S(2)}, u32[]{:S(2)}) collective-permute-start(bf16[192,512]{1,0:T(8,128)(2,1)} %param.13), channel_id=1, source_target_pairs={{0,15},{1,0},{2,1},{3,2},{4,3},{5,4},{6,5},{7,6},{8,7},{9,8},{10,9... | collective-permute-start | bytes 589832 | tf_op jit(solution)/shard_map/ppermute | solution.py:21
  23.2 4.7 %collective-permute-start.2 = (bf16[192,512]{1,0:T(8,128)(2,1)}, bf16[192,512]{1,0:T(8,128)(2,1)}, u32[]{:S(2)}, u32[]{:S(2)}) collective-permute-start(bf16[192,512]{1,0:T(8,128)(2,1)} %collective-permute-done.1), channel_id=1, source_target_pairs={{0,15},{1,0},{2,1},{3,2},{4,3},{5,4},{6,5},{7,6},{8,7},{9,8},{10,9... | collective-permute-start | bytes 589832 | tf_op jit(solution)/shard_map/ppermute | solution.py:21
  28.0 7.3 %slice.45 = f32[192,256]{1,0:T(8,128)} slice(f32[192,512]{1,0:T(8,128)S(1)} %broadcast_multiply_fusion), slice={[0:192:1], [0:512:2]} | slice | bytes 393216 | tf_op jit(solution)/shard_map/slice | solution.py:33
  39.5 4.6 %collective-permute-start.4 = (bf16[192,512]{1,0:T(8,128)(2,1)}, bf16[192,512]{1,0:T(8,128)(2,1)}, u32[]{:S(2)}, u32[]{:S(2)}) collective-permute-start(bf16[192,512]{1,0:T(8,128)(2,1)} %collective-permute-done.3), channel_id=1, source_target_pairs={{0,15},{1,0},{2,1},{3,2},{4,3},{5,4},{6,5},{7,6},{8,7},{9,8},{10,9... | collective-permute-start | bytes 589832 | tf_op jit(solution)/shard_map/ppermute | solution.py:21
  44.1 8.1 %gather_fusion = bf16[192,64,512]{2,1,0:T(8,128)(2,1)} fusion(bf16[16,64,512]{2,1,0:T(8,128)(2,1)S(1)} %copy-done.2, s32[1024]{0:T(1024)S(1)} %pad_clamp_fusion.2), kind=kCustom, calls=%fused_computation | custom fusion | bytes 25166592 | tf_op jit(solution)/shard_map/gather | solution.py:110
  63.5 4.6 %collective-permute-start.7 = (bf16[192,512]{1,0:T(8,128)(2,1)S(1)}, bf16[192,512]{1,0:T(8,128)(2,1)S(1)}, u32[]{:S(2)}, u32[]{:S(2)}) collective-permute-start(bf16[192,512]{1,0:T(8,128)(2,1)S(1)} %collective-permute-done.6), channel_id=1, source_target_pairs={{0,15},{1,0},{2,1},{3,2},{4,3},{5,4},{6,5},{7,6},{8,7},{9,8},{10,9... | collective-permute-start | bytes 589832 | tf_op jit(solution)/shard_map/ppermute | solution.py:21
  79.1 4.6 %collective-permute-start.9 = (bf16[192,512]{1,0:T(8,128)(2,1)S(1)}, bf16[192,512]{1,0:T(8,128)(2,1)S(1)}, u32[]{:S(2)}, u32[]{:S(2)}) collective-permute-start(bf16[192,512]{1,0:T(8,128)(2,1)S(1)} %collective-permute-done.8), channel_id=1, source_target_pairs={{0,15},{1,0},{2,1},{3,2},{4,3},{5,4},{6,5},{7,6},{8,7},{9,8},{10,9... | collective-permute-start | bytes 589832 | tf_op jit(solution)/shard_map/ppermute | solution.py:21
  86.8 4.6 %collective-permute-start.10 = (bf16[192,512]{1,0:T(8,128)(2,1)S(1)}, bf16[192,512]{1,0:T(8,128)(2,1)S(1)}, u32[]{:S(2)}, u32[]{:S(2)}) collective-permute-start(bf16[192,512]{1,0:T(8,128)(2,1)S(1)} %collective-permute-done.9), channel_id=1, source_target_pairs={{0,15},{1,0},{2,1},{3,2},{4,3},{5,4},{6,5},{7,6},{8,7},{9,8},{10,9... | collective-permute-start | bytes 589832 | tf_op jit(solution)/shard_map/ppermute | solution.py:21
  118.0 4.9 %collective-permute-start.14 = (bf16[192,512]{1,0:T(8,128)(2,1)S(1)}, bf16[192,512]{1,0:T(8,128)(2,1)S(1)}, u32[]{:S(2)}, u32[]{:S(2)}) collective-permute-start(bf16[192,512]{1,0:T(8,128)(2,1)S(1)} %collective-permute-done.13), channel_id=1, source_target_pairs={{0,15},{1,0},{2,1},{3,2},{4,3},{5,4},{6,5},{7,6},{8,7},{9,8},{10,9... | collective-permute-start | bytes 589832 | tf_op jit(solution)/shard_map/ppermute | solution.py:21
  150.7 6.3 %fusion.48 = f32[192,1,512]{2,1,0:T(1,128)S(1)} fusion(bf16[192,64,1]{1,2,0:T(2,128)(2,1)S(1)} %copy.154, bf16[192,64,512]{2,1,0:T(8,128)(2,1)} %gather_fusion), kind=kOutput, calls=%fused_computation.155 | convolution fusion | flops 12582912 | bytes 13000704 | tf_op jit(solution)/shard_map/gk,gkq->gq/dot_general | solution.py:111
  157.0 6.2 %convolution_add_fusion = f32[192,512]{1,0:T(8,128)S(1)} fusion(bf16[8192,512]{1,0:T(8,128)(2,1)} %param.15, f32[192,1,512]{2,1,0:T(1,128)S(1)} %fusion.48, f32[8192]{0:T(1024)S(1)} %copy-done.10, f32[192]{0:T(256)S(1)} %add_rsqrt_fusion, bf16[192,16384]{1,0:T(8,128)(2,1)} %copy-done.3, s32[]{:T(128)S(6)} %select_n.145), kind=kOutput, calls=%fused_computation.26 | convolution fusion | flops 1617002496 | bytes 12354308 | tf_op jit(solution)/shard_map/dot_general | solution.py:118
  163.2 7.2 %slice.46 = f32[192,256]{1,0:T(8,128)S(1)} slice(f32[192,512]{1,0:T(8,128)S(1)} %convolution_add_fusion), slice={[0:192:1], [1:512:2]} | slice | bytes 393216 | tf_op jit(solution)/shard_map/slice | solution.py:36
  170.4 6.7 %slice.44 = f32[192,256]{1,0:T(8,128)S(1)} slice(f32[192,512]{1,0:T(8,128)S(1)} %convolution_add_fusion), slice={[0:192:1], [0:512:2]} | slice | bytes 393216 | tf_op jit(solution)/shard_map/slice | solution.py:35
  178.6 12.3 %copy.132 = bf16[16,128,2048]{1,2,0:T(8,128)(2,1)} copy(bf16[16,128,2048]{2,1,0:T(8,128)(2,1)} %param.20) | data formatting | bytes 16777216 | tf_op args[7]
  191.5 37.6 %all-gather.6.cloned.1.call-done = bf16[192,10240]{1,0:T(8,128)(2,1)} async-done(((bf16[192,640]{1,0:T(8,128)(2,1)}), bf16[192,10240]{1,0:T(8,128)(2,1)}) %all-gather.6.cloned.1.call-update) | async-done | bytes 3932176 | tf_op jit(solution)/shard_map/all_gather | solution.py:130
  235.2 6.1 %reshape_reshape.12 = bf16[64,3,8,8,128]{4,3,2,1,0:T(8,128)(2,1)} reshape(bf16[192,16,512]{2,1,0:T(8,128)(2,1)} %slice.66) | data formatting | bytes 6291456 | tf_op jit(solution)/shard_map/reshape;reshape | solution.py:139
  260.1 7.9 %collective-permute-done.20 = f32[64,8,24]{2,1,0:T(8,128)S(1)} collective-permute-done((f32[64,8,24]{2,1,0:T(8,128)S(1)}, f32[64,8,24]{2,1,0:T(8,128)S(1)}, u32[]{:S(2)}, u32[]{:S(2)}) %collective-permute-start.20) | collective-permute-done | bytes 49184 | tf_op jit(solution)/shard_map/ppermute | solution.py:73
  270.0 5.9 %collective-permute-done.21 = f32[64,8,24]{2,1,0:T(8,128)S(1)} collective-permute-done((f32[64,8,24]{2,1,0:T(8,128)S(1)}, f32[64,8,24]{2,1,0:T(8,128)S(1)}, u32[]{:S(2)}, u32[]{:S(2)}) %collective-permute-start.21) | collective-permute-done | bytes 49184 | tf_op jit(solution)/shard_map/ppermute | solution.py:73
  278.0 11.4 %collective-permute-done.22 = f32[64,8,24]{2,1,0:T(8,128)S(1)} collective-permute-done((f32[64,8,24]{2,1,0:T(8,128)S(1)}, f32[64,8,24]{2,1,0:T(8,128)S(1)}, u32[]{:S(2)}, u32[]{:S(2)}) %collective-permute-start.22) | collective-permute-done | bytes 49184 | tf_op jit(solution)/shard_map/ppermute | solution.py:73
  290.9 5.7 %fusion.5 = f32[16,8,3,8,128]{4,3,2,1,0:T(8,128)} fusion(bf16[16,128,2,8,128]{1,4,3,2,0:T(8,128)(2,1)} %bitcast.110, f32[16,8,24,128]{3,2,1,0:T(8,128)S(1)} %get-tuple-element.20, f32[16,8,24]{2,1,0:T(8,128)S(1)} %gather_fusion.2, pred[16,128]{1,0:T(8,128)(4,1)S(1)} %fusion.26), kind=kOutput, calls=%fused_computation.21 | convolution fusion | flops 101842944 | bytes 7354368 | tf_op jit(solution)/shard_map/skqp,spkd->skqd/dot_general | solution.py:196
  321.1 7.2 %reshape.298 = f32[192,8192]{1,0:T(8,128)} reshape(f32[64,3,8,8,128]{4,3,2,1,0:T(8,128)} %bitcast.111) | data formatting | bytes 12582912 | tf_op jit(solution)/shard_map/reshape | solution.py:65
  328.2 19.5 %all-to-all-done = f32[16,16,3,516]{3,1,2,0:T(8,128)S(1)} async-done(((f32[16,16,3,516]{3,1,2,0:T(8,128)}), f32[16,16,3,516]{3,1,2,0:T(8,128)S(1)}, u32[]{:S(2)}, u32[]{:S(2)}) %all-to-all-start) | async-done | bytes 1585184 | tf_op jit(solution)/shard_map/all_to_all | solution.py:217
  361.0 53.3 %all-gather.4.cloned.1.call-done = bf16[192,8192]{1,0:T(8,128)(2,1)} async-done(((bf16[192,512]{1,0:T(8,128)(2,1)}), bf16[192,8192]{1,0:T(8,128)(2,1)}) %all-gather.4.cloned.1.call-update) | async-done | bytes 3145744 | tf_op jit(solution)/shard_map/all_gather | solution.py:245
  414.3 6.8 %convolution_convert_fusion = bf16[192,512]{1,0:T(8,128)(2,1)} fusion(bf16[192,8192]{1,0:T(8,128)(2,1)} %all-gather.4.cloned.1.call-done, bf16[8192,512]{1,0:T(8,128)(2,1)} %param.17), kind=kOutput, calls=%fused_computation.27 | convolution fusion | flops 1610711040 | bytes 11730944 | tf_op jit(solution)/shard_map/dot_general | solution.py:246
  (200 shorter events, 164.8 us)
Async XLA Ops:
  6.5 222.6 %all-gather.6.cloned.1.call-start = ((), (), s32[]{:S(2)}) async-start(), calls=%async_computation.2 | async-start | bytes 4177920 | tf_op jit(solution)/shard_map/all_gather | solution.py:130
  6.5 8.9 %collective-permute-start = (bf16[192,512]{1,0:T(8,128)(2,1)}, bf16[192,512]{1,0:T(8,128)(2,1)S(1)}, u32[]{:S(2)}, u32[]{:S(2)}) collective-permute-start(bf16[192,512]{1,0:T(8,128)(2,1)} %param.13), channel_id=1, source_target_pairs={{0,15},{1,0},{2,1},{3,2},{4,3},{5,4},{6,5},{7,6},{8,7},{9,8},{10,9... | collective-permute-start | bytes 589832 | tf_op jit(solution)/shard_map/ppermute | solution.py:21
  15.5 7.7 %collective-permute-start.1 = (bf16[192,512]{1,0:T(8,128)(2,1)S(1)}, bf16[192,512]{1,0:T(8,128)(2,1)}, u32[]{:S(2)}, u32[]{:S(2)}) collective-permute-start(bf16[192,512]{1,0:T(8,128)(2,1)S(1)} %collective-permute-done), channel_id=1, source_target_pairs={{0,15},{1,0},{2,1},{3,2},{4,3},{5,4},{6,5},{7,6},{8,7},{9,8},{10,9... | collective-permute-start | bytes 589832 | tf_op jit(solution)/shard_map/ppermute | solution.py:21
  23.2 12.1 %collective-permute-start.2 = (bf16[192,512]{1,0:T(8,128)(2,1)}, bf16[192,512]{1,0:T(8,128)(2,1)}, u32[]{:S(2)}, u32[]{:S(2)}) collective-permute-start(bf16[192,512]{1,0:T(8,128)(2,1)} %collective-permute-done.1), channel_id=1, source_target_pairs={{0,15},{1,0},{2,1},{3,2},{4,3},{5,4},{6,5},{7,6},{8,7},{9,8},{10,9... | collective-permute-start | bytes 589832 | tf_op jit(solution)/shard_map/ppermute | solution.py:21
  35.3 4.3 collective-permute-start.3
  39.5 12.7 %collective-permute-start.4 = (bf16[192,512]{1,0:T(8,128)(2,1)}, bf16[192,512]{1,0:T(8,128)(2,1)}, u32[]{:S(2)}, u32[]{:S(2)}) collective-permute-start(bf16[192,512]{1,0:T(8,128)(2,1)} %collective-permute-done.3), channel_id=1, source_target_pairs={{0,15},{1,0},{2,1},{3,2},{4,3},{5,4},{6,5},{7,6},{8,7},{9,8},{10,9... | collective-permute-start | bytes 589832 | tf_op jit(solution)/shard_map/ppermute | solution.py:21
  55.8 7.7 %collective-permute-start.6 = (bf16[192,512]{1,0:T(8,128)(2,1)S(1)}, bf16[192,512]{1,0:T(8,128)(2,1)S(1)}, u32[]{:S(2)}, u32[]{:S(2)}) collective-permute-start(bf16[192,512]{1,0:T(8,128)(2,1)S(1)} %collective-permute-done.5), channel_id=1, source_target_pairs={{0,15},{1,0},{2,1},{3,2},{4,3},{5,4},{6,5},{7,6},{8,7},{9,8},{10,9... | collective-permute-start | bytes 589832 | tf_op jit(solution)/shard_map/ppermute | solution.py:21
  63.5 7.8 %collective-permute-start.7 = (bf16[192,512]{1,0:T(8,128)(2,1)S(1)}, bf16[192,512]{1,0:T(8,128)(2,1)S(1)}, u32[]{:S(2)}, u32[]{:S(2)}) collective-permute-start(bf16[192,512]{1,0:T(8,128)(2,1)S(1)} %collective-permute-done.6), channel_id=1, source_target_pairs={{0,15},{1,0},{2,1},{3,2},{4,3},{5,4},{6,5},{7,6},{8,7},{9,8},{10,9... | collective-permute-start | bytes 589832 | tf_op jit(solution)/shard_map/ppermute | solution.py:21
  71.3 7.8 %collective-permute-start.8 = (bf16[192,512]{1,0:T(8,128)(2,1)S(1)}, bf16[192,512]{1,0:T(8,128)(2,1)S(1)}, u32[]{:S(2)}, u32[]{:S(2)}) collective-permute-start(bf16[192,512]{1,0:T(8,128)(2,1)S(1)} %collective-permute-done.7), channel_id=1, source_target_pairs={{0,15},{1,0},{2,1},{3,2},{4,3},{5,4},{6,5},{7,6},{8,7},{9,8},{10,9... | collective-permute-start | bytes 589832 | tf_op jit(solution)/shard_map/ppermute | solution.py:21
  79.1 7.8 %collective-permute-start.9 = (bf16[192,512]{1,0:T(8,128)(2,1)S(1)}, bf16[192,512]{1,0:T(8,128)(2,1)S(1)}, u32[]{:S(2)}, u32[]{:S(2)}) collective-permute-start(bf16[192,512]{1,0:T(8,128)(2,1)S(1)} %collective-permute-done.8), channel_id=1, source_target_pairs={{0,15},{1,0},{2,1},{3,2},{4,3},{5,4},{6,5},{7,6},{8,7},{9,8},{10,9... | collective-permute-start | bytes 589832 | tf_op jit(solution)/shard_map/ppermute | solution.py:21
  86.8 7.8 %collective-permute-start.10 = (bf16[192,512]{1,0:T(8,128)(2,1)S(1)}, bf16[192,512]{1,0:T(8,128)(2,1)S(1)}, u32[]{:S(2)}, u32[]{:S(2)}) collective-permute-start(bf16[192,512]{1,0:T(8,128)(2,1)S(1)} %collective-permute-done.9), channel_id=1, source_target_pairs={{0,15},{1,0},{2,1},{3,2},{4,3},{5,4},{6,5},{7,6},{8,7},{9,8},{10,9... | collective-permute-start | bytes 589832 | tf_op jit(solution)/shard_map/ppermute | solution.py:21
  94.6 7.8 %collective-permute-start.11 = (bf16[192,512]{1,0:T(8,128)(2,1)S(1)}, bf16[192,512]{1,0:T(8,128)(2,1)S(1)}, u32[]{:S(2)}, u32[]{:S(2)}) collective-permute-start(bf16[192,512]{1,0:T(8,128)(2,1)S(1)} %collective-permute-done.10), channel_id=1, source_target_pairs={{0,15},{1,0},{2,1},{3,2},{4,3},{5,4},{6,5},{7,6},{8,7},{9,8},{10,9... | collective-permute-start | bytes 589832 | tf_op jit(solution)/shard_map/ppermute | solution.py:21
  102.4 7.8 %collective-permute-start.12 = (bf16[192,512]{1,0:T(8,128)(2,1)S(1)}, bf16[192,512]{1,0:T(8,128)(2,1)S(1)}, u32[]{:S(2)}, u32[]{:S(2)}) collective-permute-start(bf16[192,512]{1,0:T(8,128)(2,1)S(1)} %collective-permute-done.11), channel_id=1, source_target_pairs={{0,15},{1,0},{2,1},{3,2},{4,3},{5,4},{6,5},{7,6},{8,7},{9,8},{10,9... | collective-permute-start | bytes 589832 | tf_op jit(solution)/shard_map/ppermute | solution.py:21
  110.2 7.8 %collective-permute-start.13 = (bf16[192,512]{1,0:T(8,128)(2,1)S(1)}, bf16[192,512]{1,0:T(8,128)(2,1)S(1)}, u32[]{:S(2)}, u32[]{:S(2)}) collective-permute-start(bf16[192,512]{1,0:T(8,128)(2,1)S(1)} %collective-permute-done.12), channel_id=1, source_target_pairs={{0,15},{1,0},{2,1},{3,2},{4,3},{5,4},{6,5},{7,6},{8,7},{9,8},{10,9... | collective-permute-start | bytes 589832 | tf_op jit(solution)/shard_map/ppermute | solution.py:21
  118.0 8.1 %collective-permute-start.14 = (bf16[192,512]{1,0:T(8,128)(2,1)S(1)}, bf16[192,512]{1,0:T(8,128)(2,1)S(1)}, u32[]{:S(2)}, u32[]{:S(2)}) collective-permute-start(bf16[192,512]{1,0:T(8,128)(2,1)S(1)} %collective-permute-done.13), channel_id=1, source_target_pairs={{0,15},{1,0},{2,1},{3,2},{4,3},{5,4},{6,5},{7,6},{8,7},{9,8},{10,9... | collective-permute-start | bytes 589832 | tf_op jit(solution)/shard_map/ppermute | solution.py:21
  132.2 5.1 %collective-permute-start.15 = (bf16[192,64]{0,1:T(8,128)(2,1)S(1)}, bf16[192,64]{0,1:T(8,128)(2,1)S(1)}, u32[]{:S(2)}, u32[]{:S(2)}) collective-permute-start(bf16[192,64]{0,1:T(8,128)(2,1)S(1)} %fusion.9), channel_id=1, source_target_pairs={{0,1},{1,0},{2,3},{3,2},{4,5},{5,4},{6,7},{7,6},{8,9},{9,8},{10,11... | collective-permute-start | bytes 73736 | tf_op jit(solution)/shard_map/ppermute | solution.py:73
  137.4 4.0 collective-permute-start.16
  141.4 4.0 collective-permute-start.17
  145.4 5.2 %collective-permute-start.18 = (bf16[192,64]{0,1:T(8,128)(2,1)S(1)}, bf16[192,64]{0,1:T(8,128)(2,1)S(1)}, u32[]{:S(2)}, u32[]{:S(2)}) collective-permute-start(bf16[192,64]{0,1:T(8,128)(2,1)S(1)} %add.194), channel_id=1, source_target_pairs={{0,8},{1,9},{2,10},{3,11},{4,12},{5,13},{6,14},{7,15},{8,0},{9,1},... | collective-permute-start | bytes 73736 | tf_op jit(solution)/shard_map/ppermute | solution.py:73
  259.5 8.5 %collective-permute-start.20 = (f32[64,8,24]{2,1,0:T(8,128)S(1)}, f32[64,8,24]{2,1,0:T(8,128)S(1)}, u32[]{:S(2)}, u32[]{:S(2)}) collective-permute-start(f32[64,8,24]{2,1,0:T(8,128)S(1)} %max.16), channel_id=1, source_target_pairs={{0,2},{1,3},{2,0},{3,1},{4,6},{5,7},{6,4},{7,5},{8,10},{9,11},{10,... | collective-permute-start | bytes 147464 | tf_op jit(solution)/shard_map/ppermute | solution.py:73
  268.0 7.9 %collective-permute-start.21 = (f32[64,8,24]{2,1,0:T(8,128)S(1)}, f32[64,8,24]{2,1,0:T(8,128)S(1)}, u32[]{:S(2)}, u32[]{:S(2)}) collective-permute-start(f32[64,8,24]{2,1,0:T(8,128)S(1)} %max.17), channel_id=1, source_target_pairs={{0,4},{1,5},{2,6},{3,7},{4,0},{5,1},{6,2},{7,3},{8,12},{9,13},{10,... | collective-permute-start | bytes 147464 | tf_op jit(solution)/shard_map/ppermute | solution.py:73
  275.9 13.5 %collective-permute-start.22 = (f32[64,8,24]{2,1,0:T(8,128)S(1)}, f32[64,8,24]{2,1,0:T(8,128)S(1)}, u32[]{:S(2)}, u32[]{:S(2)}) collective-permute-start(f32[64,8,24]{2,1,0:T(8,128)S(1)} %max.18), channel_id=1, source_target_pairs={{0,8},{1,9},{2,10},{3,11},{4,12},{5,13},{6,14},{7,15},{8,0},{9,1},... | collective-permute-start | bytes 147464 | tf_op jit(solution)/shard_map/ppermute | solution.py:73
  305.3 42.5 %all-to-all-start = ((f32[16,16,3,516]{3,1,2,0:T(8,128)}), f32[16,16,3,516]{3,1,2,0:T(8,128)S(1)}, u32[]{:S(2)}, u32[]{:S(2)}) async-start(f32[16,16,3,516]{3,1,2,0:T(8,128)} %copy.143), calls=%async_computation | async-start | bytes 3932160 | tf_op jit(solution)/shard_map/all_to_all | solution.py:217
  309.0 105.3 %all-gather.4.cloned.1.call-start = ((), (), s32[]{:S(2)}) async-start(), calls=%async_computation.1 | async-start | bytes 3342336 | tf_op jit(solution)/shard_map/all_gather | solution.py:245
  (13 other events, 367.5 us)
Sparse Core Ops, SparseCore 0:
  178.7 50.3 all-gather.5
  361.1 53.1 all-gather.3
